TPU v7x, 128 devices: a whole 4x4x4 slice. The times are simulated.
128 devices in a mesh: dp: 4 (over x), ctx: 8 (over z, core), head: 4 (over y).
Axes of the slice: x: 4, y: 4, z: 4, core: 2. Of those that a mesh axis runs over, the one named last changes fastest.
Arguments:
- token_values: bfloat16 [4, 4096, 8192], P('dp', 'ctx', 'head'), may hold values from -6 to 6
- gate_values: bfloat16 [4, 4096, 8192], P('dp', 'ctx', 'head'), may hold values from -6 to 6
- state_maps: bfloat16 [4, 4096, 8, 512], P('dp', 'ctx', 'head'), may hold values from -6 to 6
- step_raw: bfloat16 [4, 4096, 128], P('dp', 'ctx', 'head'), may hold values from -6.7 to 9.683792
- log_rate: float32 [128], P('head'), may hold values from -6 to 3
- skip_gain: float32 [128], P('head'), may hold values from 0.5 to 1.5
- conv_values: float32 [4, 8192], P(None, 'head'), may hold values from -3 to 3
- conv_maps: float32 [4, 8, 512], P(None, 'head'), may hold values from -3 to 3
- piece_shift: int32 [32], replicated, may hold values from 0 to 31, as said below
- doc_start: int32 [4, 4096], P('dp', 'ctx'), may hold values 0 or 1
- norm_gain: float32 [8192], P('head'), may hold values from 0.1 to 1.9
- out_weight: bfloat16 [8192, 4096], P('head'), may hold values from -0.0625 to 0.0625
Outputs:
- mixed: bfloat16 [4, 4096, 4096], P('dp', 'ctx', 'head')
Inputs may be any that keep to these rules, and one draw needn't show every extreme that they name: `piece_shift`: no value occurs more than 2 times and some value occurs exactly 2 times.
All inputs are finite; a program needn't handle non-finite values. No bound on the sum of `doc_start` on one device may be relied on, other than what follows from the above.
Results may differ from a plain program's by a relative error of at most 0.014.
Values may be sent and summed in bfloat16 or wider, within the bound.
No kernel may reach another device: no remote copies, remote signals or barrier semaphores. Data moves between devices by JAX's collectives and lax.ppermute only.
A program may use at most 256 MiB of HBM per device.

v0:
```python
import jax
import jax.numpy as jnp
from jax import lax
from jax.sharding import PartitionSpec as P

BLOCK_LEN = 128


eps = 1e-05


def passed_along(block, axis, distance):
    devices = range(lax.axis_size(axis))
    route = [(i - distance, i) for i in devices if i - distance in devices]
    return lax.ppermute(block, axis, route)


def chain(gate, summed, axis):
    count = lax.axis_size(axis)
    place = lax.axis_index(axis)
    core = place % 2
    chip = place // 2
    chips = count // 2
    swap = [(i, i ^ 1) for i in range(count)]

    def join(earlier, latter):
        return (earlier[0] * latter[0], latter[0][:, None, None] * earlier[1] + latter[1])

    def across(pair, route):
        gate_in, summed_in = lax.ppermute((pair[0], pair[1].astype(jnp.bfloat16)), axis, route)
        return gate_in, summed_in.astype(jnp.float32)

    local = (gate, summed)
    other = across(local, swap)
    lead = core == 0
    first = tuple(jnp.where(lead, a, b) for a, b in zip(local, other))
    second = tuple(jnp.where(lead, b, a) for a, b in zip(local, other))
    both = join(first, second)
    half = gate.shape[0] // 2
    mine = tuple(lax.dynamic_slice_in_dim(a, core * half, half, 0) for a in both)

    def fetch(pair, distance):
        gate_in, summed_in = across(pair, [(i - 2 * distance, i) for i in range(2 * distance, count)])
        return jnp.where(chip >= distance, gate_in, 1.0), summed_in

    before = fetch(mine, 1)
    window = join(before, mine)
    distance = 2
    while distance < chips:
        received = fetch(window, distance)
        before = join(received, before)
        distance *= 2
        if distance < chips:
            window = join(received, window)
    partner = across(before, swap)
    whole = tuple(
        jnp.where(lead, jnp.concatenate([a, b]), jnp.concatenate([b, a]))
        for a, b in zip(before, partner)
    )
    return jnp.where(lead, whole[1], join(whole, first)[1])


def conv_core(ext_values, weight, free_ext, length):
    tap_count = weight.shape[0]
    summed = jnp.zeros((length,) + ext_values.shape[1:], jnp.float32)
    keeping = jnp.ones((length,), jnp.float32)
    bshape = (length,) + (1,) * (ext_values.ndim - 1)
    for back in range(tap_count):
        if back > 0:
            keeping = keeping * free_ext[tap_count - back : tap_count - back + length]
        sample = ext_values[tap_count - 1 - back : tap_count - 1 - back + length].astype(
            jnp.float32
        )
        summed = summed + weight[tap_count - 1 - back] * sample * keeping.reshape(bshape)
    return jax.nn.silu(summed).astype(jnp.bfloat16)


def body(
    token_values,
    gate_values,
    state_maps,
    step_raw,
    log_rate,
    skip_gain,
    conv_values,
    conv_maps,
    piece_shift,
    doc_start,
    norm_gain,
    out_weight,
):
    owners = lax.axis_size(("dp", "ctx"))
    myself = lax.axis_index(("dp", "ctx"))
    slots = piece_shift.shape[0]
    rows = token_values.shape[1]
    piece_rows = rows // slots
    most = 2 * slots // owners
    slot_ids = jnp.arange(slots, dtype=jnp.int32)
    matching = piece_shift[:, None] == piece_shift[None, :]
    ranking = jnp.sum(
        (matching & (slot_ids[None, :] < slot_ids[:, None])).astype(jnp.int32), axis=1
    )
    offsets = (jnp.arange(owners, dtype=jnp.int32) - myself) % owners
    chosen = (piece_shift[None, None, :] == offsets[:, None, None]) & (
        ranking[None, None, :] == jnp.arange(most, dtype=jnp.int32)[None, :, None]
    )
    send_slot = jnp.sum(chosen.astype(jnp.int32) * slot_ids[None, None, :], axis=2)

    def outgoing(local):
        pieces = local[0].reshape((slots, piece_rows) + local.shape[2:])
        return pieces[send_slot]

    features = token_values.shape[2]
    map_shape = state_maps.shape[2:]
    map_width = map_shape[0] * map_shape[1]
    joined = jnp.concatenate(
        [token_values[0], state_maps[0].reshape(rows, map_width), step_raw[0]], axis=1
    )
    incoming = lax.all_to_all(
        outgoing(joined[None]), ("dp", "ctx"), split_axis=0, concat_axis=0, tiled=True
    )
    incoming_z = lax.all_to_all(
        outgoing(gate_values), ("dp", "ctx"), split_axis=0, concat_axis=0, tiled=True
    )
    source = (myself - piece_shift) % owners

    def placed(received):
        return received[source, ranking].reshape((rows,) + received.shape[3:])

    joined_pack = placed(incoming)
    margin = conv_values.shape[0] - 1
    flags = doc_start[0].astype(jnp.bfloat16)
    halo = joined[rows - margin :]
    halo_shift = (piece_shift[slots - 1] + 1) % owners
    distance = 1
    while distance < owners:
        route = [(i, (i + distance) % owners) for i in range(owners)]
        halo = lax.cond(
            (halo_shift // distance) % 2 == 1,
            lambda block, route=route: lax.ppermute(block, ("dp", "ctx"), route),
            lambda block: block,
            halo,
        )
        distance *= 2
    earlier = lax.axis_index("ctx") > 0
    rim = jnp.concatenate(
        [halo, passed_along(flags[rows - margin :], "ctx", 1)[:, None]], axis=1
    )
    rim = jnp.where(earlier, rim, jnp.zeros_like(rim))
    rim_x = rim[:, :features]
    rim_maps = rim[:, features : features + map_width].reshape((margin,) + map_shape)
    rim_flags = rim[:, -1]
    x_pack = joined_pack[:, :features]
    map_pack = joined_pack[:, features : features + map_width].reshape((rows,) + map_shape)
    dt_pack = joined_pack[:, features + map_width :]
    free_ext = 1.0 - jnp.concatenate([rim_flags, flags]).astype(jnp.float32)
    x_conv = conv_core(jnp.concatenate([rim_x, x_pack]), conv_values, free_ext, rows)
    map_conv = conv_core(jnp.concatenate([rim_maps, map_pack]), conv_maps, free_ext, rows)
    heads_local = log_rate.shape[0]
    groups_local = map_pack.shape[1]
    per_group = heads_local // groups_local
    width = x_pack.shape[1] // heads_local
    state = map_pack.shape[2] // 2
    span = BLOCK_LEN
    blocks = rows // span
    step_dt = jax.nn.softplus(dt_pack.astype(jnp.float32))
    log_decay = step_dt * (-jnp.exp(log_rate))[None, :]
    cum_t = jnp.cumsum(log_decay.reshape(blocks, span, heads_local), axis=1).transpose(0, 2, 1)
    dt_t = step_dt.reshape(blocks, span, heads_local).transpose(0, 2, 1)
    segment = jnp.cumsum(doc_start[0].reshape(blocks, span), axis=1)
    x_blocks = x_conv.reshape(blocks, span, groups_local, per_group, width)
    b_blocks = map_conv[:, :, :state].reshape(blocks, span, groups_local, state)
    c_blocks = map_conv[:, :, state:].reshape(blocks, span, groups_local, state)
    scores = jnp.einsum("bqgn,bsgn->bgqs", c_blocks, b_blocks, preferred_element_type=jnp.float32)
    later = jnp.arange(span)[:, None] >= jnp.arange(span)[None, :]
    allowed = later[None] & (segment[:, :, None] == segment[:, None, :])
    spread = cum_t[:, :, :, None] - cum_t[:, :, None, :]
    decay = jnp.exp(jnp.where(allowed[:, None], spread, -jnp.inf))
    weights = (
        decay.reshape(blocks, groups_local, per_group, span, span)
        * scores[:, :, None]
        * dt_t.reshape(blocks, groups_local, per_group, 1, span)
    ).astype(jnp.bfloat16)
    y_diag = jnp.einsum("bghts,bsghp->btghp", weights, x_blocks, preferred_element_type=jnp.float32)
    same_end = (segment == segment[:, -1:]).astype(jnp.float32)
    carry_coef = jnp.exp(cum_t[:, :, -1:] - cum_t) * dt_t * same_end[:, None, :]
    x_weighted = (
        x_blocks.astype(jnp.float32)
        * carry_coef.transpose(0, 2, 1).reshape(blocks, span, groups_local, per_group, 1)
    ).astype(jnp.bfloat16)
    block_states = jnp.einsum(
        "bsghp,bsgn->bghpn", x_weighted, b_blocks, preferred_element_type=jnp.float32
    ).reshape(blocks, heads_local, width, state)
    block_gates = jnp.exp(cum_t[:, :, -1]) * (segment[:, -1] == 0).astype(jnp.float32)[:, None]

    prior_states = [jnp.zeros_like(block_states[0])]
    prior_gates = [jnp.ones_like(block_gates[0])]
    for b in range(1, blocks):
        prior_states.append(block_gates[b - 1][:, None, None] * prior_states[-1] + block_states[b - 1])
        prior_gates.append(prior_gates[-1] * block_gates[b - 1])
    slab_state = block_gates[-1][:, None, None] * prior_states[-1] + block_states[-1]
    slab_gate = prior_gates[-1] * block_gates[-1]
    z_pack = placed(incoming_z)
    arriving = chain(slab_gate, slab_state, "ctx")
    entering = (
        (jnp.stack(prior_states) + jnp.stack(prior_gates)[:, :, None, None] * arriving[None])
        .astype(jnp.bfloat16)
        .reshape(blocks, groups_local, per_group, width, state)
    )
    y_off = jnp.einsum("bqgn,bghpn->bqghp", c_blocks, entering, preferred_element_type=jnp.float32)
    reach = (
        (jnp.exp(cum_t) * (segment == 0).astype(jnp.float32)[:, None, :])
        .transpose(0, 2, 1)
        .reshape(blocks, span, groups_local, per_group, 1)
    )
    mixed_y = (
        y_diag
        + y_off * reach
        + skip_gain.reshape(groups_local, per_group, 1) * x_blocks.astype(jnp.float32)
    )
    gated = mixed_y * jax.nn.silu(
        z_pack.astype(jnp.float32).reshape(blocks, span, groups_local, per_group, width)
    )
    power = jnp.mean(gated * gated, axis=(3, 4), keepdims=True)
    normed = (
        (gated * lax.rsqrt(power + eps) * norm_gain.reshape(groups_local, per_group, width))
        .astype(jnp.bfloat16)
        .reshape(rows, heads_local * width)
    )
    partial_value = jnp.dot(normed, out_weight, preferred_element_type=jnp.float32)
    result = lax.psum_scatter(
        partial_value.astype(jnp.bfloat16), "head", scatter_dimension=1, tiled=True
    )
    return result[None]


def solution(mesh):
    return jax.shard_map(
        body,
        mesh=mesh,
        in_specs=(
            P("dp", "ctx", "head"),
            P("dp", "ctx", "head"),
            P("dp", "ctx", "head", None),
            P("dp", "ctx", "head"),
            P("head"),
            P("head"),
            P(None, "head"),
            P(None, "head", None),
            P(),
            P("dp", "ctx"),
            P("head"),
            P("head", None),
        ),
        out_specs=P("dp", "ctx", "head"),
        check_vma=False,
    )
```

profile of v0, /device:TPU:2, one launch (start us, length us, event | category | flops | bytes accessed | tf_op | source)
XLA Modules:
  0.0 311.4 jit_solution(16153303344875212535)
XLA Ops:
  14.4 5.8 %gather_fusion = bf16[64,16,3104]{2,1,0:T(8,128)(2,1)} fusion(bf16[32,16,3104]{2,1,0:T(8,128)(2,1)} %pad_maximum_fusion, s32[1024]{0:T(1024)S(1)} %pad_clamp_fusion), kind=kCustom, calls=%fused_computation | custom fusion | bytes 12714240 | tf_op jit(solution)/shard_map/gather | solution.py:111
  20.3 8.6 %all-to-all-start = ((bf16[32,2,16,3104]{3,2,1,0:T(8,128)(2,1)}), bf16[32,2,16,3104]{3,2,1,0:T(8,128)(2,1)}, u32[]{:S(2)}, u32[]{:S(2)}) async-start(bf16[32,2,16,3104]{3,2,1,0:T(8,128)(2,1)} %bitcast.128), calls=%async_computation | async-start | bytes 13107200 | tf_op jit(solution)/shard_map/all_to_all | solution.py:119
  37.6 71.3 %conditional.6 = (bf16[3,3104]{1,0:T(4,128)(2,1)S(1)}) conditional(s32[]{:T(128)} %convert_element_type.133, bf16[3,3104]{1,0:T(4,128)(2,1)S(1)} %get-tuple-element.85, bf16[3,3104]{1,0:T(4,128)(2,1)S(1)} %get-tuple-element.85), branch_computations={%region_4.5_spmd, %region_5.6_spmd} | conditional | bytes 111792 | solution.py:138
  39.1 69.7 %collective-permute-done.1 = bf16[3,3104]{1,0:T(4,128)(2,1)S(1)} collective-permute-done((bf16[3,3104]{1,0:T(4,128)(2,1)S(1)}, bf16[3,3104]{1,0:T(4,128)(2,1)S(1)}, u32[]{:S(2)}, u32[]{:S(2)}) %collective-permute-start.1) | collective-permute-done | bytes 18656 | tf_op jit(solution)/shard_map/cond/branch_1_fun/ppermute | solution.py:140
  108.8 6.5 %conditional.7 = (bf16[3,3104]{1,0:T(4,128)(2,1)S(1)}) conditional(s32[]{:T(128)} %convert_element_type.132, bf16[3,3104]{1,0:T(4,128)(2,1)S(1)} %get-tuple-element.86, bf16[3,3104]{1,0:T(4,128)(2,1)S(1)} %get-tuple-element.86), branch_computations={%region_6.7_spmd, %region_7.8_spmd} | conditional | bytes 111792 | solution.py:138
  108.9 6.4 %collective-permute-done.2 = bf16[3,3104]{1,0:T(4,128)(2,1)S(1)} collective-permute-done((bf16[3,3104]{1,0:T(4,128)(2,1)S(1)}, bf16[3,3104]{1,0:T(4,128)(2,1)S(1)}, u32[]{:S(2)}, u32[]{:S(2)}) %collective-permute-start.2) | collective-permute-done | bytes 18656 | tf_op jit(solution)/shard_map/cond/branch_1_fun/ppermute | solution.py:140
  115.4 3.9 %conditional.8 = (bf16[3,3104]{1,0:T(4,128)(2,1)S(1)}) conditional(s32[]{:T(128)} %convert_element_type.131, bf16[3,3104]{1,0:T(4,128)(2,1)S(1)} %get-tuple-element.87, bf16[3,3104]{1,0:T(4,128)(2,1)S(1)} %get-tuple-element.87), branch_computations={%region_8.9_spmd, %region_9.10_spmd} | conditional | bytes 111792 | solution.py:138
  115.5 3.8 %collective-permute-done.3 = bf16[3,3104]{1,0:T(4,128)(2,1)S(1)} collective-permute-done((bf16[3,3104]{1,0:T(4,128)(2,1)S(1)}, bf16[3,3104]{1,0:T(4,128)(2,1)S(1)}, u32[]{:S(2)}, u32[]{:S(2)}) %collective-permute-start.3) | collective-permute-done | bytes 18656 | tf_op jit(solution)/shard_map/cond/branch_1_fun/ppermute | solution.py:140
  120.7 6.2 %all-to-all-start.1 = ((bf16[32,2,16,2048]{3,2,1,0:T(8,128)(2,1)}), bf16[32,2,16,2048]{3,2,1,0:T(8,128)(2,1)}, u32[]{:S(2)}, u32[]{:S(2)}) async-start(bf16[32,2,16,2048]{3,2,1,0:T(8,128)(2,1)} %bitcast.129), calls=%async_computation.1 | async-start | bytes 8388608 | tf_op jit(solution)/shard_map/all_to_all | solution.py:122
  127.1 5.4 %gather_fusion.1 = bf16[32,16,3104]{2,1,0:T(8,128)(2,1)} fusion(bf16[32,2,16,3104]{3,2,1,0:T(8,128)(2,1)} %all-to-all-done, s32[32]{0:T(128)S(1)} %fusion.52), kind=kCustom, calls=%fused_computation.1 | custom fusion | bytes 6357248 | tf_op jit(solution)/shard_map/gather | solution.py:128
  141.1 7.8 %multiply_convert_fusion.3 = bf16[512,2048]{1,0:T(8,128)(2,1)S(1)} fusion(bf16[512,2048]{1,0:T(8,128)(2,1)} %slice.183, bf16[3,2048]{1,0:T(4,128)(2,1)S(1)} %slice-done, f32[512]{0:T(512)S(1)} %get-tuple-element.47, f32[2048]{0:T(1024)S(1)} %bitcast.156, f32[512]{0:T(512)S(1)} %get-tuple-element.48, f32[2048]{0:T(1024)S(1)} %bitcast.157, ...), kind=kLoop, calls=%fused_computation.23 | loop fusion | flops 29360128 | bytes 4245504 | tf_op jit(solution)/shard_map/convert_element_type | solution.py:75
  148.9 5.3 %reshape.329 = bf16[4,128,2,16,64]{4,3,2,1,0:T(8,128)(2,1)} reshape(bf16[512,2048]{1,0:T(8,128)(2,1)S(1)} %multiply_convert_fusion.3) | data formatting | bytes 4194304 | tf_op jit(solution)/shard_map/reshape | solution.py:171
  154.2 5.6 %copy.98 = bf16[4,128,2,16,64]{1,4,3,2,0:T(8,128)(2,1)S(1)} copy(bf16[4,128,2,16,64]{4,3,2,1,0:T(8,128)(2,1)} %reshape.329) | data formatting | bytes 4194304 | tf_op jit(solution)/shard_map/reshape | solution.py:171
  162.1 4.6 %fusion.16 = f32[4,2,16,64,256]{4,3,2,1,0:T(8,128)} fusion(bf16[4,128,2,16,64]{1,4,3,2,0:T(8,128)(2,1)S(1)} %copy.98, f32[4,128,2,16]{1,3,2,0:T(8,128)S(1)} %get-tuple-element.59, bf16[4,128,2,256,1]{3,1,0,2,4:T(8,128)(2,1)S(1)} %bitcast.135), kind=kOutput, calls=%fused_computation.31 | convolution fusion | flops 540016640 | bytes 11075584 | tf_op jit(solution)/shard_map/bsghp,bsgn->bghpn/dot_general | solution.py:191
  166.8 7.9 %multiply_add_fusion = (f32[1,2,16,64,256]{4,3,2,1,0:T(8,128)}, f32[1,2,16,64,256]{4,3,2,1,0:T(8,128)}, f32[1,2,16,64,256]{4,3,2,1,0:T(8,128)}, f32[1,2,16,64,25...) fusion(f32[2,16]{1,0:T(2,128)S(1)} %mul.481, ...), kind=kLoop, calls=%fused_computation.44 | loop fusion | flops 2621440 | bytes 23069056 | tf_op jit(solution)/shard_map/add | solution.py:199
  174.7 3.7 %fusion.59 = (bf16[32,64,256]{2,1,0:T(8,128)(2,1)S(1)}, f32[32,64,256]{2,1,0:T(8,128)}) fusion(f32[1,2,16,64,256]{4,3,2,1,0:T(8,128)} %get-tuple-element.52, f32[1,2,16,64,256]{4,3,2,1,0:T(8,128)S(1)} %get-tuple-element.51, f32[1,2,16,64,256]{4,3,2,1,0:T(8,128)S(1)} %get-tuple-element.50, f32[1,2,16,64,256]{4,3,2,1,0:T(8,128)S(1)} %get-tuple-element.49, ...), kind=kLoop, calls=%fused_computation.150 | loop fusion | flops 4194304 | bytes 11534848 | tf_op jit(solution)/shard_map/convert_element_type | solution.py:30
  185.1 4.4 %collective-permute-start.9 = (bf16[16,64,256]{2,1,0:T(8,128)(2,1)}, bf16[16,64,256]{2,1,0:T(8,128)(2,1)}, u32[]{:S(2)}, u32[]{:S(2)}) collective-permute-start(bf16[16,64,256]{2,1,0:T(8,128)(2,1)} %get-tuple-element.40), channel_id=1, source_target_pairs={{0,8},{4,12},{8,16},{12,20},{16,24},{20,28},{1,9},{5,13},{9,17},{1... | collective-permute-start | bytes 1572872 | tf_op jit(solution)/shard_map/ppermute | solution.py:30
  189.8 4.2 %gather_fusion.3 = bf16[32,16,2048]{2,1,0:T(8,128)(2,1)} fusion(bf16[32,2,16,2048]{3,2,1,0:T(8,128)(2,1)} %all-to-all-done.1, s32[32]{0:T(128)S(1)} %fusion.52), kind=kCustom, calls=%fused_computation.3 | custom fusion | bytes 4194560 | tf_op jit(solution)/shard_map/gather | solution.py:128
  194.1 7.4 %reshape.291 = f32[4,128,2,16,64]{4,3,2,1,0:T(8,128)} reshape(bf16[32,16,2048]{2,1,0:T(8,128)(2,1)} %gather_fusion.3) | data formatting | bytes 6291456 | tf_op jit(solution)/shard_map/convert_element_type | solution.py:222
  201.4 8.0 %copy.106 = f32[4,128,2,16,64]{1,4,3,2,0:T(8,128)} copy(f32[4,128,2,16,64]{4,3,2,1,0:T(8,128)} %reshape.291) | data formatting | bytes 8388608 | tf_op jit(solution)/shard_map/convert_element_type | solution.py:222
  211.8 4.6 %collective-permute-start.10 = (bf16[16,64,256]{2,1,0:T(8,128)(2,1)}, bf16[16,64,256]{2,1,0:T(8,128)(2,1)}, u32[]{:S(2)}, u32[]{:S(2)}) collective-permute-start(bf16[16,64,256]{2,1,0:T(8,128)(2,1)} %fusion.29), channel_id=1, source_target_pairs={{0,16},{4,20},{8,24},{12,28},{1,17},{5,21},{9,25},{13,29},{2,18},{... | collective-permute-start | bytes 1572872 | tf_op jit(solution)/shard_map/ppermute | solution.py:30
  221.5 5.6 %collective-permute-done.7 = f32[16]{0:T(128)S(1)} collective-permute-done((f32[16]{0:T(128)S(1)}, f32[16]{0:T(128)S(1)}, u32[]{:S(2)}, u32[]{:S(2)}) %collective-permute-start.7) | collective-permute-done | bytes 96 | tf_op jit(solution)/shard_map/ppermute | solution.py:30
  241.2 13.9 %convolution_convert_fusion = bf16[512,4096]{1,0:T(8,128)(2,1)} fusion(bf16[2048,4096]{1,0:T(8,128)(2,1)} %param.33, bf16[256,8,4,128]{3,2,1,0:T(4,128)(2,1)S(1)} %bitcast.146), kind=kOutput, calls=%fused_computation.7 | convolution fusion | flops 8592031744 | bytes 23068672 | tf_op jit(solution)/shard_map/dot_general | solution.py:230
  255.2 49.4 %reduce-scatter.2.cloned.1.call-done = bf16[512,1024]{1,0:T(8,128)(2,1)} async-done(((bf16[512,4096]{1,0:T(8,128)(2,1)}), bf16[512,1024]{1,0:T(8,128)(2,1)}) %reduce-scatter.2.cloned.1.call-update) | async-done | bytes 1048592 | tf_op jit(solution)/shard_map/reduce_scatter | solution.py:231
  (149 shorter events, 58.1 us)
Async XLA Ops:
  6.5 27.4 %copy-start = (bf16[1,512,2048]{2,1,0:T(8,128)(2,1)S(1)}, bf16[1,512,2048]{2,1,0:T(8,128)(2,1)}, u32[]{:S(2)}) copy-start(bf16[1,512,2048]{2,1,0:T(8,128)(2,1)} %param.23) | copy-start | bytes 6291460
  20.3 8.7 %copy-start.15 = (s32[1,512]{1,0:T(1,128)S(1)}, s32[1,512]{1,0:T(1,128)}, u32[]{:S(2)}) copy-start(s32[1,512]{1,0:T(1,128)} %param.31) | copy-start | bytes 6148
  20.3 10.8 %copy-start.18 = (s32[32]{0:T(128)S(1)}, s32[32]{0:T(128)}, u32[]{:S(2)}) copy-start(s32[32]{0:T(128)} %param.30) | copy-start | bytes 388
  20.3 12.2 %copy-start.6 = (bf16[1,512,2,512]{3,2,1,0:T(2,128)(2,1)S(1)}, bf16[1,512,2,512]{3,2,1,0:T(2,128)(2,1)}, u32[]{:S(2)}) copy-start(bf16[1,512,2,512]{3,2,1,0:T(2,128)(2,1)} %param.24) | copy-start | bytes 3145732
  20.3 100.4 %all-to-all-start = ((bf16[32,2,16,3104]{3,2,1,0:T(8,128)(2,1)}), bf16[32,2,16,3104]{3,2,1,0:T(8,128)(2,1)}, u32[]{:S(2)}, u32[]{:S(2)}) async-start(bf16[32,2,16,3104]{3,2,1,0:T(8,128)(2,1)} %bitcast.128), calls=%async_computation | async-start | bytes 13107200 | tf_op jit(solution)/shard_map/all_to_all | solution.py:119
  29.0 90.9 %collective-permute-start.5 = (bf16[3]{0:T(256)(128)(2,1)S(1)}, bf16[3]{0:T(256)(128)(2,1)S(1)}, u32[]{:S(2)}, u32[]{:S(2)}) collective-permute-start(bf16[3]{0:T(256)(128)(2,1)S(1)} %slice_bitcast_fusion.4), channel_id=1, source_target_pairs={{0,4},{4,8},{8,12},{12,16},{16,20},{20,24},{24,28},{1,5},{5,9},{9,... | collective-permute-start | bytes 26 | tf_op jit(solution)/shard_map/ppermute | solution.py:15
  36.7 83.0 %copy-start.19 = (f32[32]{0:T(128)S(1)}, f32[32]{0:T(128)}, u32[]{:S(2)}) copy-start(f32[32]{0:T(128)} %param.26) | copy-start | bytes 388
  36.7 83.1 %copy-start.16 = (f32[4,2,512]{2,1,0:T(2,128)S(1)}, f32[4,2,512]{2,1,0:T(2,128)}, u32[]{:S(2)}) copy-start(f32[4,2,512]{2,1,0:T(2,128)} %param.29) | copy-start | bytes 49156
  36.7 83.1 %copy-start.14 = (f32[4,2048]{1,0:T(4,128)S(1)}, f32[4,2048]{1,0:T(4,128)}, u32[]{:S(2)}) copy-start(f32[4,2048]{1,0:T(4,128)} %param.28) | copy-start | bytes 98308
  37.6 71.3 %collective-permute-start.1 = (bf16[3,3104]{1,0:T(4,128)(2,1)S(1)}, bf16[3,3104]{1,0:T(4,128)(2,1)S(1)}, u32[]{:S(2)}, u32[]{:S(2)}) collective-permute-start(bf16[3,3104]{1,0:T(4,128)(2,1)S(1)} %param.3), channel_id=1, source_target_pairs={{0,8},{4,12},{8,16},{12,20},{16,24},{20,28},{24,32},{28,36},{32,40... | collective-permute-start | bytes 55880 | tf_op jit(solution)/shard_map/cond/branch_1_fun/ppermute | solution.py:140
  108.9 6.5 %collective-permute-start.2 = (bf16[3,3104]{1,0:T(4,128)(2,1)S(1)}, bf16[3,3104]{1,0:T(4,128)(2,1)S(1)}, u32[]{:S(2)}, u32[]{:S(2)}) collective-permute-start(bf16[3,3104]{1,0:T(4,128)(2,1)S(1)} %param.5), channel_id=1, source_target_pairs={{0,16},{4,20},{8,24},{12,28},{16,32},{20,36},{24,40},{28,44},{32,4... | collective-permute-start | bytes 55880 | tf_op jit(solution)/shard_map/cond/branch_1_fun/ppermute | solution.py:140
  115.4 3.9 %collective-permute-start.3 = (bf16[3,3104]{1,0:T(4,128)(2,1)S(1)}, bf16[3,3104]{1,0:T(4,128)(2,1)S(1)}, u32[]{:S(2)}, u32[]{:S(2)}) collective-permute-start(bf16[3,3104]{1,0:T(4,128)(2,1)S(1)} %param.7), channel_id=1, source_target_pairs={{0,32},{4,36},{8,40},{12,44},{16,48},{20,52},{24,56},{28,60},{32,6... | collective-permute-start | bytes 55880 | tf_op jit(solution)/shard_map/cond/branch_1_fun/ppermute | solution.py:140
  120.7 69.2 %all-to-all-start.1 = ((bf16[32,2,16,2048]{3,2,1,0:T(8,128)(2,1)}), bf16[32,2,16,2048]{3,2,1,0:T(8,128)(2,1)}, u32[]{:S(2)}, u32[]{:S(2)}) async-start(bf16[32,2,16,2048]{3,2,1,0:T(8,128)(2,1)} %bitcast.129), calls=%async_computation.1 | async-start | bytes 8388608 | tf_op jit(solution)/shard_map/all_to_all | solution.py:122
  126.9 177.7 %reduce-scatter.2.cloned.1.call-start = ((), (), s32[]{:S(2)}) async-start(), calls=%async_computation.3 | async-start | bytes 5242880 | tf_op jit(solution)/shard_map/reduce_scatter | solution.py:231
  159.8 6.9 %copy-start.3 = (bf16[4,128,2,16,64]{1,4,3,2,0:T(8,128)(2,1)}, bf16[4,128,2,16,64]{1,4,3,2,0:T(8,128)(2,1)S(1)}, u32[]{:S(2)}) copy-start(bf16[4,128,2,16,64]{1,4,3,2,0:T(8,128)(2,1)S(1)} %copy.98) | copy-start | bytes 6291460
  178.4 2.7 collective-permute-start.8
  178.5 2.5 collective-permute-start.6
  183.7 5.9 %copy-start.17 = (f32[2048]{0:T(1024)S(1)}, f32[2048]{0:T(1024)}, u32[]{:S(2)}) copy-start(f32[2048]{0:T(1024)} %param.32) | copy-start | bytes 24580
  185.1 24.4 %collective-permute-start.9 = (bf16[16,64,256]{2,1,0:T(8,128)(2,1)}, bf16[16,64,256]{2,1,0:T(8,128)(2,1)}, u32[]{:S(2)}, u32[]{:S(2)}) collective-permute-start(bf16[16,64,256]{2,1,0:T(8,128)(2,1)} %get-tuple-element.40), channel_id=1, source_target_pairs={{0,8},{4,12},{8,16},{12,20},{16,24},{20,28},{1,9},{5,13},{9,17},{1... | collective-permute-start | bytes 1572872 | tf_op jit(solution)/shard_map/ppermute | solution.py:30
  211.8 15.3 %collective-permute-start.10 = (bf16[16,64,256]{2,1,0:T(8,128)(2,1)}, bf16[16,64,256]{2,1,0:T(8,128)(2,1)}, u32[]{:S(2)}, u32[]{:S(2)}) collective-permute-start(bf16[16,64,256]{2,1,0:T(8,128)(2,1)} %fusion.29), channel_id=1, source_target_pairs={{0,16},{4,20},{8,24},{12,28},{1,17},{5,21},{9,25},{13,29},{2,18},{... | collective-permute-start | bytes 1572872 | tf_op jit(solution)/shard_map/ppermute | solution.py:30
  220.1 7.0 %collective-permute-start.7 = (f32[16]{0:T(128)S(1)}, f32[16]{0:T(128)S(1)}, u32[]{:S(2)}, u32[]{:S(2)}) collective-permute-start(f32[16]{0:T(128)S(1)} %dynamic_slice.6), channel_id=1, source_target_pairs={{0,8},{4,12},{8,16},{12,20},{16,24},{20,28},{1,9},{5,13},{9,17},{1... | collective-permute-start | bytes 200 | tf_op jit(solution)/shard_map/ppermute | solution.py:30
  221.5 7.2 %copy-start.4 = (bf16[4,128,2,16,64]{1,4,3,2,0:T(8,128)(2,1)S(1)}, bf16[4,128,2,16,64]{1,4,3,2,0:T(8,128)(2,1)}, u32[]{:S(2)}) copy-start(bf16[4,128,2,16,64]{1,4,3,2,0:T(8,128)(2,1)} %copy-done.3) | copy-start | bytes 6291460
  228.6 3.8 %collective-permute-start.11 = (bf16[16,64,256]{2,1,0:T(8,128)(2,1)S(1)}, bf16[16,64,256]{2,1,0:T(8,128)(2,1)S(1)}, u32[]{:S(2)}, u32[]{:S(2)}) collective-permute-start(bf16[16,64,256]{2,1,0:T(8,128)(2,1)S(1)} %get-tuple-element.35), channel_id=1, source_target_pairs={{0,4},{4,0},{8,12},{12,8},{16,20},{20,16},{24,28},{28,24},{1,5},{5... | collective-permute-start | bytes 1572872 | tf_op jit(solution)/shard_map/ppermute | solution.py:30
  255.2 49.4 %copy-start.1 = (bf16[1,512,2048]{2,1,0:T(8,128)(2,1)S(1)}, bf16[1,512,2048]{2,1,0:T(8,128)(2,1)}, u32[]{:S(2)}) copy-start(bf16[1,512,2048]{2,1,0:T(8,128)(2,1)} %param.23) | copy-start | bytes 6291460
  (11 other events, 29.4 us)
Sparse Core Ops, SparseCore 0:
  255.3 49.2 reduce-scatter.1
where the time goes:
time: 313 us; the launch traced here: 311 us
  waiting for transfers between devices  137 us (44%)
  local copies, waits for them, and re-layouts  64.6 us (21%)
  other arithmetic  38.7 us (12%)
  starting transfers between devices  29.6 us (9%)
  matrix products  26.6 us (8%)
  between operations  14.7 us (5%)
    ppermute x3, waiting for transfers between devices, body(): lax.ppermute(block, ('dp', 'ctx'), route)  79.9 us
    reduce_scatter x1, waiting for transfers between devices, body(): lax.psum_scatter(partial_value.astype(jnp.bfloat16), 'head', scatter_dime...  49.4 us
    convert_element_type x2, local copies, waits for them, and re-layouts, body(): z_pack.astype(jnp.float32)  15.4 us
    dot_general x1, matrix products, body(): jnp.dot(normed, out_weight, preferred_element_type=jnp.float32)  13.9 us
    reshape x2, local copies, waits for them, and re-layouts, body(): x_blocks = x_conv.reshape(blocks, span, groups_local, per_group, width)  10.9 us
    ppermute x6, starting transfers between devices, across(): lax.ppermute((pair[0], pair[1].astype(jnp.bfloat16)), axis, route)  10.9 us
    convert_element_type x2, other arithmetic, conv_core(): return jax.nn.silu(summed).astype(jnp.bfloat16)  10.2 us
    gather x2, local copies, waits for them, and re-layouts, placed(): return received[source, ranking].reshape((rows,) + received.shape[3:])  9.6 us
  transfers between devices with their start and end apart: 13, of which 6 were waited for; matrix products, arithmetic and copies ran while one was open for 29% of the time, Pallas kernels for 0%

commit v1 on v0

--- a/solution.py
+++ b/solution.py
@@ -213,14 +213,12 @@
         .transpose(0, 2, 1)
         .reshape(blocks, span, groups_local, per_group, 1)
     )
-    mixed_y = (
-        y_diag
-        + y_off * reach
-        + skip_gain.reshape(groups_local, per_group, 1) * x_blocks.astype(jnp.float32)
-    )
-    gated = mixed_y * jax.nn.silu(
+    ready_y = y_diag + skip_gain.reshape(groups_local, per_group, 1) * x_blocks.astype(jnp.float32)
+    gate_act = jax.nn.silu(
         z_pack.astype(jnp.float32).reshape(blocks, span, groups_local, per_group, width)
     )
+    ready_y, gate_act = lax.optimization_barrier((ready_y, gate_act))
+    gated = (ready_y + y_off * reach) * gate_act
     power = jnp.mean(gated * gated, axis=(3, 4), keepdims=True)
     normed = (
         (gated * lax.rsqrt(power + eps) * norm_gain.reshape(groups_local, per_group, width))

time: 313 us -> 319 us (1.019)
  other arithmetic: 38.7 us -> 51.1 us
  waiting for transfers between devices: 137 us -> 133 us
  local copies, waits for them, and re-layouts: 64.6 us -> 61 us
    mul x0 -> x1, other arithmetic: none -> 5.42 us  [body(): jax.nn.silu(z_pack.astype(jnp.float32).reshape(blocks, span, groups_local...]
    ppermute x6, waiting for transfers between devices: 7.81 us -> 3.23 us  [across(): lax.ppermute((pair[0], pair[1].astype(jnp.bfloat16)), axis, route)]
    dot_general x1, matrix products: 3.68 us -> 7.22 us  [body(): jnp.einsum('bghts,bsghp->btghp', weights, x_blocks, preferred_element_typ...]
  transfers between devices with their start and end apart: 13 -> 13, of which waited for: 6 -> 6; matrix products, arithmetic and copies ran while one was open for 29% -> 30% of each run, Pallas kernels for 0% -> 0%
where the time goes in v1:
time: 319 us; the launch traced here: 318 us
  waiting for transfers between devices  133 us (42%)
  local copies, waits for them, and re-layouts  61 us (19%)
  other arithmetic  51.1 us (16%)
  starting transfers between devices  29.6 us (9%)
  matrix products  28.6 us (9%)
  between operations  14.7 us (5%)
    ppermute x3, waiting for transfers between devices, body(): lax.ppermute(block, ('dp', 'ctx'), route)  80 us
    reduce_scatter x1, waiting for transfers between devices, body(): lax.psum_scatter(partial_value.astype(jnp.bfloat16), 'head', scatter_dime...  49.4 us
    convert_element_type x2, local copies, waits for them, and re-layouts, body(): z_pack.astype(jnp.float32)  13.7 us
    dot_general x1, matrix products, body(): jnp.dot(normed, out_weight, preferred_element_type=jnp.float32)  11 us
    reshape x2, local copies, waits for them, and re-layouts, body(): x_blocks = x_conv.reshape(blocks, span, groups_local, per_group, width)  10.9 us
    ppermute x6, starting transfers between devices, across(): lax.ppermute((pair[0], pair[1].astype(jnp.bfloat16)), axis, route)  10.8 us
    convert_element_type x2, other arithmetic, conv_core(): return jax.nn.silu(summed).astype(jnp.bfloat16)  10.4 us
    convert_element_type x4, other arithmetic, across(): pair[1].astype(jnp.bfloat16)  9.93 us
  transfers between devices with their start and end apart: 13, of which 6 were waited for; matrix products, arithmetic and copies ran while one was open for 30% of the time, Pallas kernels for 0%

profile of v1, /device:TPU:2, one launch (start us, length us, event | category | flops | bytes accessed | tf_op | source)
XLA Modules:
  0.0 317.7 jit_solution(8159778429803754820)
XLA Ops:
  14.4 5.9 %gather_fusion = bf16[64,16,3104]{2,1,0:T(8,128)(2,1)} fusion(bf16[32,16,3104]{2,1,0:T(8,128)(2,1)} %pad_maximum_fusion, s32[1024]{0:T(1024)S(1)} %pad_clamp_fusion), kind=kCustom, calls=%fused_computation | custom fusion | bytes 12714240 | tf_op jit(solution)/shard_map/gather | solution.py:111
  20.3 8.6 %all-to-all-start = ((bf16[32,2,16,3104]{3,2,1,0:T(8,128)(2,1)}), bf16[32,2,16,3104]{3,2,1,0:T(8,128)(2,1)}, u32[]{:S(2)}, u32[]{:S(2)}) async-start(bf16[32,2,16,3104]{3,2,1,0:T(8,128)(2,1)} %bitcast.129), calls=%async_computation | async-start | bytes 13107200 | tf_op jit(solution)/shard_map/all_to_all | solution.py:119
  37.6 71.3 %conditional.6 = (bf16[3,3104]{1,0:T(4,128)(2,1)S(1)}) conditional(s32[]{:T(128)} %convert_element_type.133, bf16[3,3104]{1,0:T(4,128)(2,1)S(1)} %get-tuple-element.89, bf16[3,3104]{1,0:T(4,128)(2,1)S(1)} %get-tuple-element.89), branch_computations={%region_4.5_spmd, %region_5.6_spmd} | conditional | bytes 111792 | solution.py:138
  39.2 69.7 %collective-permute-done.1 = bf16[3,3104]{1,0:T(4,128)(2,1)S(1)} collective-permute-done((bf16[3,3104]{1,0:T(4,128)(2,1)S(1)}, bf16[3,3104]{1,0:T(4,128)(2,1)S(1)}, u32[]{:S(2)}, u32[]{:S(2)}) %collective-permute-start.1) | collective-permute-done | bytes 18656 | tf_op jit(solution)/shard_map/cond/branch_1_fun/ppermute | solution.py:140
  108.9 6.5 %conditional.7 = (bf16[3,3104]{1,0:T(4,128)(2,1)S(1)}) conditional(s32[]{:T(128)} %convert_element_type.132, bf16[3,3104]{1,0:T(4,128)(2,1)S(1)} %get-tuple-element.90, bf16[3,3104]{1,0:T(4,128)(2,1)S(1)} %get-tuple-element.90), branch_computations={%region_6.7_spmd, %region_7.8_spmd} | conditional | bytes 111792 | solution.py:138
  109.0 6.4 %collective-permute-done.2 = bf16[3,3104]{1,0:T(4,128)(2,1)S(1)} collective-permute-done((bf16[3,3104]{1,0:T(4,128)(2,1)S(1)}, bf16[3,3104]{1,0:T(4,128)(2,1)S(1)}, u32[]{:S(2)}, u32[]{:S(2)}) %collective-permute-start.2) | collective-permute-done | bytes 18656 | tf_op jit(solution)/shard_map/cond/branch_1_fun/ppermute | solution.py:140
  115.4 3.9 %conditional.8 = (bf16[3,3104]{1,0:T(4,128)(2,1)S(1)}) conditional(s32[]{:T(128)} %convert_element_type.131, bf16[3,3104]{1,0:T(4,128)(2,1)S(1)} %get-tuple-element.91, bf16[3,3104]{1,0:T(4,128)(2,1)S(1)} %get-tuple-element.91), branch_computations={%region_8.9_spmd, %region_9.10_spmd} | conditional | bytes 111792 | solution.py:138
  115.5 3.8 %collective-permute-done.3 = bf16[3,3104]{1,0:T(4,128)(2,1)S(1)} collective-permute-done((bf16[3,3104]{1,0:T(4,128)(2,1)S(1)}, bf16[3,3104]{1,0:T(4,128)(2,1)S(1)}, u32[]{:S(2)}, u32[]{:S(2)}) %collective-permute-start.3) | collective-permute-done | bytes 18656 | tf_op jit(solution)/shard_map/cond/branch_1_fun/ppermute | solution.py:140
  120.7 6.2 %all-to-all-start.1 = ((bf16[32,2,16,2048]{3,2,1,0:T(8,128)(2,1)}), bf16[32,2,16,2048]{3,2,1,0:T(8,128)(2,1)}, u32[]{:S(2)}, u32[]{:S(2)}) async-start(bf16[32,2,16,2048]{3,2,1,0:T(8,128)(2,1)} %bitcast.130), calls=%async_computation.1 | async-start | bytes 8388608 | tf_op jit(solution)/shard_map/all_to_all | solution.py:122
  127.2 5.4 %gather_fusion.1 = bf16[32,16,3104]{2,1,0:T(8,128)(2,1)} fusion(bf16[32,2,16,3104]{3,2,1,0:T(8,128)(2,1)} %all-to-all-done, s32[32]{0:T(128)S(1)} %fusion.52), kind=kCustom, calls=%fused_computation.1 | custom fusion | bytes 6357248 | tf_op jit(solution)/shard_map/gather | solution.py:128
  141.2 7.9 %multiply_convert_fusion.3 = bf16[512,2048]{1,0:T(8,128)(2,1)S(1)} fusion(bf16[512,2048]{1,0:T(8,128)(2,1)} %slice.183, bf16[3,2048]{1,0:T(4,128)(2,1)S(1)} %slice-done, f32[512]{0:T(512)S(1)} %get-tuple-element.51, f32[2048]{0:T(1024)S(1)} %bitcast.156, f32[512]{0:T(512)S(1)} %get-tuple-element.52, f32[2048]{0:T(1024)S(1)} %bitcast.157, ...), kind=kLoop, calls=%fused_computation.24 | loop fusion | flops 29360128 | bytes 4245504 | tf_op jit(solution)/shard_map/convert_element_type | solution.py:75
  149.1 5.3 %reshape.329 = bf16[4,128,2,16,64]{4,3,2,1,0:T(8,128)(2,1)} reshape(bf16[512,2048]{1,0:T(8,128)(2,1)S(1)} %multiply_convert_fusion.3) | data formatting | bytes 4194304 | tf_op jit(solution)/shard_map/reshape | solution.py:171
  154.4 5.6 %copy.98 = bf16[4,128,2,16,64]{1,4,3,2,0:T(8,128)(2,1)S(1)} copy(bf16[4,128,2,16,64]{4,3,2,1,0:T(8,128)(2,1)} %reshape.329) | data formatting | bytes 4194304 | tf_op jit(solution)/shard_map/reshape | solution.py:171
  164.0 4.5 %fusion.16 = f32[4,2,16,64,256]{4,3,2,1,0:T(8,128)} fusion(bf16[4,128,2,16,64]{1,4,3,2,0:T(8,128)(2,1)S(1)} %copy.98, f32[4,128,2,16]{1,3,2,0:T(8,128)S(1)} %get-tuple-element.63, bf16[4,128,2,256,1]{3,1,0,2,4:T(8,128)(2,1)S(1)} %bitcast.136), kind=kOutput, calls=%fused_computation.32 | convolution fusion | flops 540016640 | bytes 11075584 | tf_op jit(solution)/shard_map/bsghp,bsgn->bghpn/dot_general | solution.py:191
  168.5 7.9 %multiply_add_fusion = (f32[1,2,16,64,256]{4,3,2,1,0:T(8,128)}, f32[1,2,16,64,256]{4,3,2,1,0:T(8,128)}, f32[1,2,16,64,256]{4,3,2,1,0:T(8,128)}, f32[1,2,16,64,25...) fusion(f32[2,16]{1,0:T(2,128)S(1)} %mul.485, ...), kind=kLoop, calls=%fused_computation.45 | loop fusion | flops 2621440 | bytes 23069056 | tf_op jit(solution)/shard_map/add | solution.py:199
  187.3 4.2 %collective-permute-start.9 = (bf16[16,64,256]{2,1,0:T(8,128)(2,1)}, bf16[16,64,256]{2,1,0:T(8,128)(2,1)}, u32[]{:S(2)}, u32[]{:S(2)}) collective-permute-start(bf16[16,64,256]{2,1,0:T(8,128)(2,1)} %get-tuple-element.44), channel_id=1, source_target_pairs={{0,8},{4,12},{8,16},{12,20},{16,24},{20,28},{1,9},{5,13},{9,17},{1... | collective-permute-start | bytes 1572872 | tf_op jit(solution)/shard_map/ppermute | solution.py:30
  195.3 5.6 %reshape.290 = f32[4,128,2,16,64]{4,3,2,1,0:T(8,128)} reshape(bf16[32,16,2048]{2,1,0:T(8,128)(2,1)S(1)} %gather_fusion.3) | data formatting | bytes 6291456 | tf_op jit(solution)/shard_map/convert_element_type | solution.py:218
  200.9 8.1 %copy.101 = f32[4,128,2,16,64]{1,4,3,2,0:T(8,128)} copy(f32[4,128,2,16,64]{4,3,2,1,0:T(8,128)} %reshape.290) | data formatting | bytes 8388608 | tf_op jit(solution)/shard_map/convert_element_type | solution.py:218
  211.1 4.8 %collective-permute-start.10 = (bf16[16,64,256]{2,1,0:T(8,128)(2,1)}, bf16[16,64,256]{2,1,0:T(8,128)(2,1)}, u32[]{:S(2)}, u32[]{:S(2)}) collective-permute-start(bf16[16,64,256]{2,1,0:T(8,128)(2,1)} %fusion.29), channel_id=1, source_target_pairs={{0,16},{4,20},{8,24},{12,28},{1,17},{5,21},{9,25},{13,29},{2,18},{... | collective-permute-start | bytes 1572872 | tf_op jit(solution)/shard_map/ppermute | solution.py:30
  215.8 5.4 %divide_multiply_fusion = f32[4,128,2,16,64]{1,4,3,2,0:T(8,128)} fusion(f32[4,128,2,16,64]{1,4,3,2,0:T(8,128)} %copy.101), kind=kLoop, calls=%fused_computation.18 | loop fusion | flops 4194304 | bytes 8388608 | tf_op jit(solution)/shard_map/jit(silu)/mul | solution.py:217
  229.2 7.2 %fusion.2 = f32[4,128,2,16,64]{1,4,3,2,0:T(8,128)} fusion(bf16[4,128,2,16,64]{1,4,3,2,0:T(8,128)(2,1)S(1)} %copy-done.6, f32[4,2,16,128]{3,2,1,0:T(8,128)S(1)} %bitcast.153, f32[4,2,128,128]{3,2,1,0:T(8,128)S(1)} %copy-done.13, f32[4,2,16,128]{3,2,1,0:T(8,128)} %bitcast.152, pred[4,128,128]{2,1,0:T(8,128)(4,1)} %compare_and_fusion, f32[2,16]{1,0:T(2,128)S(1)} %mul.466), kind=kOutput, calls=%fused_computation.11 | convolution fusion | flops 282066944 | bytes 7012480 | tf_op jit(solution)/shard_map/bghts,bsghp->btghp/dot_general | solution.py:184
  241.8 4.7 %multiply_reduce_fusion = (f32[4,128,2]{1,2,0:T(2,128)S(1)}, f32[4,128,2,16,64]{1,4,3,2,0:T(8,128)S(1)}) fusion(f32[4,128,2,16,64]{1,4,3,2,0:T(8,128)S(1)} %copy-done.2, f32[4,128,2,16,64]{1,4,3,2,0:T(8,128)} %fusion.2, f32[4,128,2,16]{1,3,2,0:T(8,128)S(1)} %get-tuple-element.64, bf16[4,128,2,256,1]{3,1,0,2,4:T(8,128)(2,1)S(1)} %bitcast.139, ...), kind=kOutput, calls=%fused_computation.17 | convolution fusion | flops 554695680 | bytes 21565968 | tf_op jit(solution)/shard_map/bqgn,bghpn->bqghp/dot_general | solution.py:210
  250.4 11.0 %convolution_convert_fusion = bf16[512,4096]{1,0:T(8,128)(2,1)} fusion(bf16[2048,4096]{1,0:T(8,128)(2,1)S(1)} %bitcast.161, bf16[256,8,4,128]{3,2,1,0:T(4,128)(2,1)S(1)} %bitcast.146), kind=kOutput, calls=%fused_computation.7 | convolution fusion | flops 8592031744 | bytes 23068672 | tf_op jit(solution)/shard_map/dot_general | solution.py:228
  261.4 49.4 %reduce-scatter.2.cloned.1.call-done = bf16[512,1024]{1,0:T(8,128)(2,1)} async-done(((bf16[512,4096]{1,0:T(8,128)(2,1)}), bf16[512,1024]{1,0:T(8,128)(2,1)}) %reduce-scatter.2.cloned.1.call-update) | async-done | bytes 1048592 | tf_op jit(solution)/shard_map/reduce_scatter | solution.py:229
  (163 shorter events, 65.2 us)
Async XLA Ops:
  6.5 27.5 %copy-start = (bf16[1,512,2048]{2,1,0:T(8,128)(2,1)S(1)}, bf16[1,512,2048]{2,1,0:T(8,128)(2,1)}, u32[]{:S(2)}) copy-start(bf16[1,512,2048]{2,1,0:T(8,128)(2,1)} %param.23) | copy-start | bytes 6291460
  20.3 8.7 %copy-start.17 = (s32[1,512]{1,0:T(1,128)S(1)}, s32[1,512]{1,0:T(1,128)}, u32[]{:S(2)}) copy-start(s32[1,512]{1,0:T(1,128)} %param.31) | copy-start | bytes 6148
  20.3 10.8 %copy-start.20 = (s32[32]{0:T(128)S(1)}, s32[32]{0:T(128)}, u32[]{:S(2)}) copy-start(s32[32]{0:T(128)} %param.30) | copy-start | bytes 388
  20.3 12.2 %copy-start.8 = (bf16[1,512,2,512]{3,2,1,0:T(2,128)(2,1)S(1)}, bf16[1,512,2,512]{3,2,1,0:T(2,128)(2,1)}, u32[]{:S(2)}) copy-start(bf16[1,512,2,512]{3,2,1,0:T(2,128)(2,1)} %param.24) | copy-start | bytes 3145732
  20.3 100.4 %all-to-all-start = ((bf16[32,2,16,3104]{3,2,1,0:T(8,128)(2,1)}), bf16[32,2,16,3104]{3,2,1,0:T(8,128)(2,1)}, u32[]{:S(2)}, u32[]{:S(2)}) async-start(bf16[32,2,16,3104]{3,2,1,0:T(8,128)(2,1)} %bitcast.129), calls=%async_computation | async-start | bytes 13107200 | tf_op jit(solution)/shard_map/all_to_all | solution.py:119
  29.1 90.9 %collective-permute-start.5 = (bf16[3]{0:T(256)(128)(2,1)S(1)}, bf16[3]{0:T(256)(128)(2,1)S(1)}, u32[]{:S(2)}, u32[]{:S(2)}) collective-permute-start(bf16[3]{0:T(256)(128)(2,1)S(1)} %slice_bitcast_fusion.4), channel_id=1, source_target_pairs={{0,4},{4,8},{8,12},{12,16},{16,20},{20,24},{24,28},{1,5},{5,9},{9,... | collective-permute-start | bytes 26 | tf_op jit(solution)/shard_map/ppermute | solution.py:15
  36.8 83.0 %copy-start.21 = (f32[32]{0:T(128)S(1)}, f32[32]{0:T(128)}, u32[]{:S(2)}) copy-start(f32[32]{0:T(128)} %param.26) | copy-start | bytes 388
  36.8 83.1 %copy-start.18 = (f32[4,2,512]{2,1,0:T(2,128)S(1)}, f32[4,2,512]{2,1,0:T(2,128)}, u32[]{:S(2)}) copy-start(f32[4,2,512]{2,1,0:T(2,128)} %param.29) | copy-start | bytes 49156
  36.8 83.1 %copy-start.16 = (f32[4,2048]{1,0:T(4,128)S(1)}, f32[4,2048]{1,0:T(4,128)}, u32[]{:S(2)}) copy-start(f32[4,2048]{1,0:T(4,128)} %param.28) | copy-start | bytes 98308
  37.6 71.3 %collective-permute-start.1 = (bf16[3,3104]{1,0:T(4,128)(2,1)S(1)}, bf16[3,3104]{1,0:T(4,128)(2,1)S(1)}, u32[]{:S(2)}, u32[]{:S(2)}) collective-permute-start(bf16[3,3104]{1,0:T(4,128)(2,1)S(1)} %param.3), channel_id=1, source_target_pairs={{0,8},{4,12},{8,16},{12,20},{16,24},{20,28},{24,32},{28,36},{32,40... | collective-permute-start | bytes 55880 | tf_op jit(solution)/shard_map/cond/branch_1_fun/ppermute | solution.py:140
  108.9 6.5 %collective-permute-start.2 = (bf16[3,3104]{1,0:T(4,128)(2,1)S(1)}, bf16[3,3104]{1,0:T(4,128)(2,1)S(1)}, u32[]{:S(2)}, u32[]{:S(2)}) collective-permute-start(bf16[3,3104]{1,0:T(4,128)(2,1)S(1)} %param.5), channel_id=1, source_target_pairs={{0,16},{4,20},{8,24},{12,28},{16,32},{20,36},{24,40},{28,44},{32,4... | collective-permute-start | bytes 55880 | tf_op jit(solution)/shard_map/cond/branch_1_fun/ppermute | solution.py:140
  115.4 3.9 %collective-permute-start.3 = (bf16[3,3104]{1,0:T(4,128)(2,1)S(1)}, bf16[3,3104]{1,0:T(4,128)(2,1)S(1)}, u32[]{:S(2)}, u32[]{:S(2)}) collective-permute-start(bf16[3,3104]{1,0:T(4,128)(2,1)S(1)} %param.7), channel_id=1, source_target_pairs={{0,32},{4,36},{8,40},{12,44},{16,48},{20,52},{24,56},{28,60},{32,6... | collective-permute-start | bytes 55880 | tf_op jit(solution)/shard_map/cond/branch_1_fun/ppermute | solution.py:140
  120.7 71.7 %all-to-all-start.1 = ((bf16[32,2,16,2048]{3,2,1,0:T(8,128)(2,1)}), bf16[32,2,16,2048]{3,2,1,0:T(8,128)(2,1)}, u32[]{:S(2)}, u32[]{:S(2)}) async-start(bf16[32,2,16,2048]{3,2,1,0:T(8,128)(2,1)} %bitcast.130), calls=%async_computation.1 | async-start | bytes 8388608 | tf_op jit(solution)/shard_map/all_to_all | solution.py:122
  127.0 183.9 %reduce-scatter.2.cloned.1.call-start = ((), (), s32[]{:S(2)}) async-start(), calls=%async_computation.3 | async-start | bytes 5242880 | tf_op jit(solution)/shard_map/reduce_scatter | solution.py:229
  160.0 8.5 %copy-start.5 = (bf16[4,128,2,16,64]{1,4,3,2,0:T(8,128)(2,1)}, bf16[4,128,2,16,64]{1,4,3,2,0:T(8,128)(2,1)S(1)}, u32[]{:S(2)}) copy-start(bf16[4,128,2,16,64]{1,4,3,2,0:T(8,128)(2,1)S(1)} %copy.98) | copy-start | bytes 6291460
  180.2 2.7 collective-permute-start.8
  180.3 2.5 collective-permute-start.6
  187.3 21.7 %collective-permute-start.9 = (bf16[16,64,256]{2,1,0:T(8,128)(2,1)}, bf16[16,64,256]{2,1,0:T(8,128)(2,1)}, u32[]{:S(2)}, u32[]{:S(2)}) collective-permute-start(bf16[16,64,256]{2,1,0:T(8,128)(2,1)} %get-tuple-element.44), channel_id=1, source_target_pairs={{0,8},{4,12},{8,16},{12,20},{16,24},{20,28},{1,9},{5,13},{9,17},{1... | collective-permute-start | bytes 1572872 | tf_op jit(solution)/shard_map/ppermute | solution.py:30
  200.9 8.2 %copy-start.11 = (f32[16,64,256]{2,1,0:T(8,128)S(1)}, f32[16,64,256]{2,1,0:T(8,128)}, u32[]{:S(2)}) copy-start(f32[16,64,256]{2,1,0:T(8,128)} %get-tuple-element.45) | copy-start | bytes 3145732
  211.1 10.9 %copy-start.12 = (bf16[512,2,256]{0,2,1:T(8,128)(2,1)S(1)}, bf16[512,2,256]{0,2,1:T(8,128)(2,1)}, u32[]{:S(2)}) copy-start(bf16[512,2,256]{0,2,1:T(8,128)(2,1)} %get-tuple-element.59) | copy-start | bytes 1572868
  211.1 15.5 %collective-permute-start.10 = (bf16[16,64,256]{2,1,0:T(8,128)(2,1)}, bf16[16,64,256]{2,1,0:T(8,128)(2,1)}, u32[]{:S(2)}, u32[]{:S(2)}) collective-permute-start(bf16[16,64,256]{2,1,0:T(8,128)(2,1)} %fusion.29), channel_id=1, source_target_pairs={{0,16},{4,20},{8,24},{12,28},{1,17},{5,21},{9,25},{13,29},{2,18},{... | collective-permute-start | bytes 1572872 | tf_op jit(solution)/shard_map/ppermute | solution.py:30
  223.3 3.2 %collective-permute-start.7 = (f32[16]{0:T(128)S(1)}, f32[16]{0:T(128)S(1)}, u32[]{:S(2)}, u32[]{:S(2)}) collective-permute-start(f32[16]{0:T(128)S(1)} %dynamic_slice.6), channel_id=1, source_target_pairs={{0,8},{4,12},{8,16},{12,20},{16,24},{20,28},{1,9},{5,13},{9,17},{1... | collective-permute-start | bytes 200 | tf_op jit(solution)/shard_map/ppermute | solution.py:30
  229.1 7.4 %collective-permute-start.11 = (bf16[16,64,256]{2,1,0:T(8,128)(2,1)}, bf16[16,64,256]{2,1,0:T(8,128)(2,1)}, u32[]{:S(2)}, u32[]{:S(2)}) collective-permute-start(bf16[16,64,256]{2,1,0:T(8,128)(2,1)} %get-tuple-element.39), channel_id=1, source_target_pairs={{0,4},{4,0},{8,12},{12,8},{16,20},{20,16},{24,28},{28,24},{1,5},{5... | collective-permute-start | bytes 1572872 | tf_op jit(solution)/shard_map/ppermute | solution.py:30
  261.4 49.5 %copy-start.1 = (bf16[1,512,2048]{2,1,0:T(8,128)(2,1)S(1)}, bf16[1,512,2048]{2,1,0:T(8,128)(2,1)}, u32[]{:S(2)}) copy-start(bf16[1,512,2048]{2,1,0:T(8,128)(2,1)} %param.23) | copy-start | bytes 6291460
  (17 other events, 73.2 us)
Sparse Core Ops, SparseCore 0:
  261.5 49.2 reduce-scatter.1
